TPU v7x, 32 devices: a whole 2x2x4 slice. The times are simulated.
32 devices in a mesh: region: 2 (over y), tile: 4 (over z), corner: 2 (over x), kern: 2 (over core).
Axes of the slice: x: 2, y: 2, z: 4, core: 2. Of those that a mesh axis runs over, the one named last changes fastest.
Arguments:
- tile_mask: bfloat16 [16, 256, 256], P(('region', 'tile')), parts along dimension 0, may hold values from -1 to 1
- master_mask: bfloat16 [8, 256, 256], P(('region', 'tile')), parts along dimension 0, may hold values from -1 to 1
- target: bfloat16 [16, 256, 256], P(('region', 'tile')), parts along dimension 0, may hold values from 0 to 1
- inst_master: int32 [16], P(('region', 'tile')), parts along dimension 0, may hold values from 0 to 3, as said below
- inst_shift: int32 [16, 2], P(('region', 'tile')), parts along dimension 0, may hold values from 0 to 255
- kernels: float32 [2, 12, 2, 32, 32], P('corner'), may hold values from -24 to 24
- kernel_weight: float32 [2, 12], P('corner'), may hold values from 0.05 to 1
- corner_dose: float32 [2], P('corner'), may hold values from 0.6 to 1.6
Outputs:
- tile_grad: float32 [16, 256, 256], P(('region', 'tile')), parts along dimension 0
- master_grad: float32 [8, 256, 256], P(('region', 'tile')), parts along dimension 0
There are 2 independent parts, one for each index of `region`. A program takes and returns all parts, laid end to end along the dimension named above; an argument that names none is the same for every part. Nothing has to cross between parts.
Inputs may be any that keep to these rules, and one draw needn't show every extreme that they name: `inst_master`: each master cell is placed in exactly 2 tiles.
All inputs are finite; a program needn't handle non-finite values.
Results may differ from a plain program's by a relative error of at most 0.0003.
Values may be sent and summed in bfloat16 or wider, within the bound.
No kernel may reach another device: no remote copies, remote signals or barrier semaphores. Data moves between devices by JAX's collectives and lax.ppermute only.
A program may use at most 64 MiB of HBM per device.

v0:
```python
import math
import jax
import jax.numpy as jnp
from jax import lax
from jax.sharding import PartitionSpec as P

P_SIZE = 256
B = 32
precise = lax.Precision.HIGHEST
steepness = 3.0
threshold = 1.0


def band_tables():
    freq = jnp.arange(B, dtype=jnp.int32) - B // 2
    pixel = jnp.arange(P_SIZE, dtype=jnp.int32)
    angle = (
        2.0 * math.pi / P_SIZE * jnp.mod(freq[:, None] * pixel[None, :], P_SIZE).astype(jnp.float32)
    )
    return (jnp.cos(angle), -jnp.sin(angle))


def phase_ramp(shift):
    freq = jnp.arange(B, dtype=jnp.int32) - B // 2
    total = (
        freq[None, :, None] * shift[:, 0][:, None, None]
        + freq[None, None, :] * shift[:, 1][:, None, None]
    )
    angle = 2.0 * math.pi / P_SIZE * jnp.mod(total, P_SIZE).astype(jnp.float32)
    return (jnp.cos(angle), -jnp.sin(angle))


def spectra(masks, cos_tab, sin_tab):
    rows_re = jnp.einsum("bx,nxy->nby", cos_tab, masks, precision=precise)
    rows_im = jnp.einsum("bx,nxy->nby", sin_tab, masks, precision=precise)
    spec_re = jnp.einsum("nby,cy->nbc", rows_re, cos_tab, precision=precise) - jnp.einsum(
        "nby,cy->nbc", rows_im, sin_tab, precision=precise
    )
    spec_im = jnp.einsum("nby,cy->nbc", rows_re, sin_tab, precision=precise) + jnp.einsum(
        "nby,cy->nbc", rows_im, cos_tab, precision=precise
    )
    return (spec_re, spec_im)


def to_field(x_re, x_im, cos_tab, sin_tab, scale):
    half_re = jnp.einsum("bx,nbc->nxc", cos_tab, x_re, precision=precise) + jnp.einsum(
        "bx,nbc->nxc", sin_tab, x_im, precision=precise
    )
    half_im = jnp.einsum("bx,nbc->nxc", cos_tab, x_im, precision=precise) - jnp.einsum(
        "bx,nbc->nxc", sin_tab, x_re, precision=precise
    )
    out_re = (
        jnp.einsum("nxc,cy->nxy", half_re, cos_tab, precision=precise)
        + jnp.einsum("nxc,cy->nxy", half_im, sin_tab, precision=precise)
    ) * scale
    out_im = (
        jnp.einsum("nxc,cy->nxy", half_im, cos_tab, precision=precise)
        - jnp.einsum("nxc,cy->nxy", half_re, sin_tab, precision=precise)
    ) * scale
    return (out_re, out_im)


def back_pixels(x_re, x_im, cos_tab, sin_tab):
    half_re = jnp.einsum("bx,nbc->nxc", cos_tab, x_re, precision=precise) + jnp.einsum(
        "bx,nbc->nxc", sin_tab, x_im, precision=precise
    )
    half_im = jnp.einsum("bx,nbc->nxc", cos_tab, x_im, precision=precise) - jnp.einsum(
        "bx,nbc->nxc", sin_tab, x_re, precision=precise
    )
    return jnp.einsum("nxc,cy->nxy", half_re, cos_tab, precision=precise) + jnp.einsum(
        "nxc,cy->nxy", half_im, sin_tab, precision=precise
    )


def adjoint(g_re, g_im, cos_tab, sin_tab, scale):
    mid_re = jnp.einsum("bx,nxy->nby", cos_tab, g_re, precision=precise) - jnp.einsum(
        "bx,nxy->nby", sin_tab, g_im, precision=precise
    )
    mid_im = jnp.einsum("bx,nxy->nby", cos_tab, g_im, precision=precise) + jnp.einsum(
        "bx,nxy->nby", sin_tab, g_re, precision=precise
    )
    out_re = (
        jnp.einsum("nby,cy->nbc", mid_re, cos_tab, precision=precise)
        - jnp.einsum("nby,cy->nbc", mid_im, sin_tab, precision=precise)
    ) * scale
    out_im = (
        jnp.einsum("nby,cy->nbc", mid_re, sin_tab, precision=precise)
        + jnp.einsum("nby,cy->nbc", mid_im, cos_tab, precision=precise)
    ) * scale
    return (out_re, out_im)


def on_device(
    tile_mask, master_mask, target, inst_master, inst_shift, kernels, kernel_weight, corner_dose
):
    cos_tab, sin_tab = band_tables()
    scale = 1.0 / (P_SIZE * P_SIZE)
    local_tiles = tile_mask.shape[0]
    tile_re, tile_im = spectra(tile_mask.astype(jnp.float32), cos_tab, sin_tab)
    ph_re, ph_im = phase_ramp(inst_shift)

    def picker(count):
        index = jnp.arange(count, dtype=jnp.int32)
        return (inst_master[:, None] == index[None, :]).astype(jnp.float32)

    piece = lax.all_gather(master_mask, "tile", axis=0, tiled=True)
    chosen = picker(piece.shape[0])
    placed = jnp.einsum("tr,rxy->txy", chosen, piece.astype(jnp.float32), precision=precise)
    sel_re, sel_im = spectra(placed, cos_tab, sin_tab)
    spec_re = tile_re + (ph_re * sel_re - ph_im * sel_im)
    spec_im = tile_im + (ph_re * sel_im + ph_im * sel_re)
    goal = target.astype(jnp.float32)
    dose = corner_dose[0]
    kern_count = lax.axis_size("kern")
    kern_pos = lax.axis_index("kern")
    per_dev = kernels.shape[1] // kern_count
    first = kern_pos * per_dev
    mine_kern = lax.dynamic_slice_in_dim(kernels[0], first, per_dev, 0)
    kern_re = mine_kern[:, 0]
    kern_im = mine_kern[:, 1]
    weights = lax.dynamic_slice_in_dim(kernel_weight[0], first, per_dev, 0)

    def make_field(h_re, h_im):
        x_re = h_re * spec_re - h_im * spec_im
        x_im = h_re * spec_im + h_im * spec_re
        return to_field(x_re, x_im, cos_tab, sin_tab, scale)

    def forward(total, item):
        h_re, h_im, weight = item
        f_re, f_im = make_field(h_re, h_im)
        return (total + weight * (f_re * f_re + f_im * f_im), None)

    partial_light, unused = lax.scan(
        forward, jnp.zeros((local_tiles, P_SIZE, P_SIZE), jnp.float32), (kern_re, kern_im, weights)
    )
    intensity = lax.psum(partial_light, "kern")
    resist = jax.nn.sigmoid(steepness * (dose * intensity - threshold))
    sens = 2.0 * (resist - goal) * resist * (1.0 - resist) * steepness * dose

    def backward(acc, item):
        h_re, h_im, weight = item
        f_re, f_im = make_field(h_re, h_im)
        g_re = 2.0 * weight * sens * f_re
        g_im = 2.0 * weight * sens * f_im
        x_re, x_im = adjoint(g_re, g_im, cos_tab, sin_tab, scale)
        return ((acc[0] + h_re * x_re + h_im * x_im, acc[1] + h_re * x_im - h_im * x_re), None)

    zero = jnp.zeros((local_tiles, B, B), jnp.float32)
    grads, unused = lax.scan(backward, (zero, zero), (kern_re, kern_im, weights))
    partial_grad = jnp.stack([grads[0], grads[1]], axis=1)
    summed = lax.psum(partial_grad, ("corner", "kern"))
    tile_grad = back_pixels(summed[:, 0], summed[:, 1], cos_tab, sin_tab)
    back_re = ph_re * summed[:, 0] + ph_im * summed[:, 1]
    back_im = ph_re * summed[:, 1] - ph_im * summed[:, 0]
    masters_all = lax.axis_size("tile") * master_mask.shape[0]
    owner_pick = picker(masters_all)
    terms = jnp.stack(
        [
            jnp.einsum("tm,tbc->mbc", owner_pick, back_re, precision=precise),
            jnp.einsum("tm,tbc->mbc", owner_pick, back_im, precision=precise),
        ],
        axis=1,
    )
    mine = lax.psum_scatter(terms, "tile", scatter_dimension=0, tiled=True)
    master_grad = back_pixels(mine[:, 0], mine[:, 1], cos_tab, sin_tab)
    return (tile_grad, master_grad)


def solution(mesh):
    return jax.shard_map(
        on_device,
        mesh=mesh,
        in_specs=(
            P(("region", "tile"), None, None),
            P(("region", "tile"), None, None),
            P(("region", "tile"), None, None),
            P(("region", "tile")),
            P(("region", "tile"), None),
            P("corner", None, None, None, None),
            P("corner", None),
            P("corner"),
        ),
        out_specs=(P(("region", "tile"), None, None), P(("region", "tile"), None, None)),
        check_vma=False,
    )
```

profile of v0, /device:TPU:0, one launch (start us, length us, event | category | flops | bytes accessed | tf_op | source)
XLA Modules:
  0.0 199.7 jit_solution(11332372084410168777)
XLA Ops:
  7.2 17.7 %all_gather.3 = bf16[4,256,256]{2,1,0:T(8,128)(2,1)S(1)} all-gather(bf16[1,256,256]{2,1,0:T(8,128)(2,1)} %param.13), channel_id=1, replica_groups=mesh['region'=2,'tile'=4,'corner'=2,'kern'=2] {'tile'}, dimensions={0}, use_global_device_ids=true | all-gather | bytes 655360 | tf_op jit(solution)/shard_map/all_gather | solution.py:106
  31.6 0.6 copy-done.7
  32.3 37.9 %while.30 = (s32[]{:T(128)}, f32[2,256,256]{2,1,0:T(8,128)S(1)}, f32[6]{0:T(128)S(1)}, f32[6,32,32]{2,1,0:T(8,128)S(1)}, f32[2,32,32]{1,2,0:T(8,128)S(1)}, /*ind...) while((s32[]{:T(128)}, f32[2,256,256]{2,1,0:T(8,128)S(1)}, ...), condition=%wide.region_1.2_spmd.clone.clone.clone.clone, body=%wide.region_0.1_spmd.clone.clone.clone.clone.sunk | while | flops 228810752 | bytes 4981891 | solution.py:133
  33.3 0.8 fusion.461
  34.9 0.8 fusion.464
  35.7 0.8 fusion.465
  37.0 1.6 fusion.466
  39.6 0.8 fusion.461
  41.2 0.8 fusion.464
  42.0 0.8 fusion.465
  43.3 1.6 fusion.466
  46.0 0.8 fusion.461
  47.5 0.8 fusion.464
  48.3 0.8 fusion.465
  49.7 1.6 fusion.466
  52.3 0.8 fusion.461
  53.9 0.8 fusion.464
  54.6 0.8 fusion.465
  56.0 1.6 fusion.466
  58.6 0.8 fusion.461
  60.2 0.8 fusion.464
  61.0 0.8 fusion.465
  62.3 1.6 fusion.466
  64.9 0.8 fusion.461
  66.5 0.8 fusion.464
  67.3 0.8 fusion.465
  68.6 1.6 fusion.466
  70.3 0.8 copy-done.1
  72.0 19.7 %all-reduce.2.cloned.1.call-done = f32[2,256,256]{2,1,0:T(8,128)} async-done(((f32[2,256,256]{2,1,0:T(8,128)}), f32[2,256,256]{2,1,0:T(8,128)}) %all-reduce.2.cloned.1.call-update) | async-done | bytes 524304 | tf_op jit(solution)/shard_map/psum | solution.py:136
  91.7 1.3 multiply_multiply_fusion
  93.0 61.6 %while.31 = (s32[]{:T(128)}, f32[2,32,32]{2,1,0:T(8,128)S(1)}, f32[2,32,32]{2,1,0:T(8,128)S(1)}, f32[6]{0:T(128)S(1)}, f32[2,256,256]{2,1,0:T(8,128)S(1)}, /*ind...) while((s32[]{:T(128)}, f32[2,32,32]{2,1,0:T(8,128)S(1)}, ...), condition=%wide.region_4.5_spmd.clone.clone.clone.clone, body=%wide.region_3.4_spmd.clone.clone.clone.clone.sunk | while | flops 456050688 | bytes 7833771 | solution.py:149
  94.0 0.8 fusion.501
  96.8 0.8 fusion.502
  98.2 0.8 fusion.496
  99.0 0.8 fusion.499
  101.0 0.6 fusion.503
  104.3 0.8 fusion.501
  107.1 0.8 fusion.502
  108.5 0.8 fusion.496
  109.3 0.8 fusion.499
  111.3 0.6 fusion.503
  114.6 0.8 fusion.501
  117.4 0.8 fusion.502
  118.8 0.8 fusion.496
  119.5 0.8 fusion.499
  124.8 0.8 fusion.501
  127.6 0.8 fusion.502
  129.0 0.8 fusion.496
  129.8 0.8 fusion.499
  135.1 0.8 fusion.501
  137.9 0.8 fusion.502
  139.3 0.8 fusion.496
  140.1 0.8 fusion.499
  145.4 0.8 fusion.501
  148.2 0.8 fusion.502
  149.6 0.8 fusion.496
  150.4 0.8 fusion.499
  154.7 12.2 %psum.15 = f32[2,2,32,32]{3,2,0,1:T(8,128)S(1)} all-reduce(f32[2,2,32,32]{3,2,0,1:T(8,128)S(1)} %pad_maximum_fusion.1), channel_id=1, replica_groups=mesh['region'=2,'tile'=4,'corner'=2,'kern'=2] {'corner','kern'}, use_global_device_ids=true, to_apply=%region_5.6 | all-reduce | flops 4096 | bytes 32768 | tf_op jit(solution)/shard_map/psum | solution.py:151
  168.6 0.7 copy.38
  170.1 0.8 fusion.219
  170.9 1.6 convolution_add_fusion.6
  172.5 16.2 %reduce-scatter.2.cloned.1.call-done = f32[1,2,32,32]{3,2,1,0:T(8,128)} async-done(((f32[4,2,32,32]{3,2,1,0:T(8,128)}), f32[1,2,32,32]{3,2,1,0:T(8,128)}) %reduce-scatter.2.cloned.1.call-update) | async-done | bytes 8208 | tf_op jit(solution)/shard_map/reduce_scatter | solution.py:164
  188.7 1.1 fusion.250
  191.6 1.3 fusion.189
  (197 shorter events, 62.4 us)
Async XLA Ops:
  7.2 24.4 %copy-start = (f32[1,12,2,32,32]{4,3,2,1,0:T(8,128)S(1)}, f32[1,12,2,32,32]{4,3,2,1,0:T(8,128)}, u32[]{:S(2)}) copy-start(f32[1,12,2,32,32]{4,3,2,1,0:T(8,128)} %param.17) | copy-start | bytes 294916
  7.2 84.5 %all-reduce.2.cloned.1.call-start = ((), (), s32[]{:S(2)}) async-start(), calls=%async_computation.1 | async-start | bytes 1048576 | tf_op jit(solution)/shard_map/psum | solution.py:136
  7.2 17.7 %copy-start.4 = (s32[2]{0:T(128)S(1)}, s32[2]{0:T(128)}, u32[]{:S(2)}) copy-start(s32[2]{0:T(128)} %param.15) | copy-start | bytes 28
  26.7 1.0 copy-start.2
  29.7 0.7 copy-start.5
  31.6 0.7 copy-start.7
  70.3 0.8 copy-start.1
  70.3 21.4 %copy-start.3 = (bf16[2,256,256]{2,1,0:T(8,128)(2,1)S(1)}, bf16[2,256,256]{2,1,0:T(8,128)(2,1)}, u32[]{:S(2)}) copy-start(bf16[2,256,256]{2,1,0:T(8,128)(2,1)} %param.14) | copy-start | bytes 786436
  71.1 117.6 %reduce-scatter.2.cloned.1.call-start = ((), (), s32[]{:S(2)}) async-start(), calls=%async_computation.2 | async-start | bytes 163840 | tf_op jit(solution)/shard_map/reduce_scatter | solution.py:164
  188.7 1.2 copy-start.6
Sparse Core Ops, SparseCore 0:
  71.2 20.4 all-reduce.1
  169.5 19.2 reduce-scatter.1
where the time goes:
time: 200 us
  matrix products  99.7 us (50%)
  waiting for transfers between devices  36 us (18%)
  blocking collectives  29.9 us (15%)
  between operations  15 us (8%)
  local copies, waits for them, and re-layouts  11.7 us (6%)
  loops' own time  5.29 us (3%)
    psum x1, waiting for transfers between devices, on_device(): intensity = lax.psum(partial_light, 'kern')  19.7 us
    all_gather x1, blocking collectives, on_device(): piece = lax.all_gather(master_mask, 'tile', axis=0, tiled=True)  17.7 us
    reduce_scatter x1, waiting for transfers between devices, on_device(): mine = lax.psum_scatter(terms, 'tile', scatter_dimension=0, tiled=True)  16.2 us
    dot_general x12, matrix products, to_field(): jnp.einsum('nxc,cy->nxy', half_im, sin_tab, precision=precise)  14.3 us
    psum x1, blocking collectives, on_device(): summed = lax.psum(partial_grad, ('corner', 'kern'))  12.2 us
    dot_general x12, matrix products, to_field(): jnp.einsum('nxc,cy->nxy', half_re, sin_tab, precision=precise)  9.2 us
    dot_general x12, matrix products, to_field(): jnp.einsum('nxc,cy->nxy', half_im, cos_tab, precision=precise)  9.12 us
    dot_general x12, matrix products, to_field(): jnp.einsum('nxc,cy->nxy', half_re, cos_tab, precision=precise)  9.1 us
  transfers between devices with their start and end apart: 2, of which 2 were waited for; matrix products, arithmetic and copies ran while one was open for 2% of the time, Pallas kernels for 0%

commit v1 on v0

--- a/solution.py
+++ b/solution.py
@@ -103,7 +103,22 @@
         index = jnp.arange(count, dtype=jnp.int32)
         return (inst_master[:, None] == index[None, :]).astype(jnp.float32)
 
-    piece = lax.all_gather(master_mask, "tile", axis=0, tiled=True)
+    ways, here, step = (lax.axis_size("tile"), lax.axis_index("tile"), master_mask.shape[0])
+    shape = [n * ways if d == 0 else n for d, n in enumerate(master_mask.shape)]
+    piece = lax.dynamic_update_slice_in_dim(
+        jnp.zeros(shape, master_mask.dtype), master_mask, here * step, axis=0
+    )
+    going_up = going_down = master_mask
+    for far in range(1, ways // 2 + 1):
+        going_up = lax.ppermute(going_up, "tile", [(d, (d + 1) % ways) for d in range(ways)])
+        piece = lax.dynamic_update_slice_in_dim(piece, going_up, (here - far) % ways * step, axis=0)
+        if 2 * far < ways:
+            going_down = lax.ppermute(
+                going_down, "tile", [(d, (d - 1) % ways) for d in range(ways)]
+            )
+            piece = lax.dynamic_update_slice_in_dim(
+                piece, going_down, (here + far) % ways * step, axis=0
+            )
     chosen = picker(piece.shape[0])
     placed = jnp.einsum("tr,rxy->txy", chosen, piece.astype(jnp.float32), precision=precise)
     sel_re, sel_im = spectra(placed, cos_tab, sin_tab)

time: 200 us -> 204 us (1.020)
  blocking collectives: 29.9 us -> 12.2 us
  local copies, waits for them, and re-layouts: 11.7 us -> 25.4 us
  starting transfers between devices: 0.26 us -> 5.43 us
    all_gather x1 -> x0, blocking collectives: 17.7 us -> none  [on_device(): piece = lax.all_gather(master_mask, 'tile', axis=0, tiled=True)]
    dynamic_update_slice x0 -> x4, local copies, waits for them, and re-layouts: none -> 13.5 us  [the longest x2 6.75 us: on_device(): lax.dynamic_update_slice_in_dim(piece, going_up, (here - far) % ways * st...]
    ppermute x0 -> x3, starting transfers between devices: none -> 5.17 us  [the longest x2 3.08 us: on_device(): lax.ppermute(going_up, 'tile', [(d, (d + 1) % ways) for d in range(ways)])]
  transfers between devices with their start and end apart: 2 -> 5, of which waited for: 2 -> 3; matrix products, arithmetic and copies ran while one was open for 2% -> 8% of each run, Pallas kernels for 0% -> 0%
where the time goes in v1:
time: 204 us; the launch traced here: 203 us
  matrix products  101 us (50%)
  waiting for transfers between devices  37.4 us (18%)
  local copies, waits for them, and re-layouts  25.4 us (12%)
  between operations  15.2 us (7%)
  blocking collectives  12.2 us (6%)
  starting transfers between devices  5.43 us (3%)
  loops' own time  5.29 us (3%)
    psum x1, waiting for transfers between devices, on_device(): intensity = lax.psum(partial_light, 'kern')  19.7 us
    reduce_scatter x1, waiting for transfers between devices, on_device(): mine = lax.psum_scatter(terms, 'tile', scatter_dimension=0, tiled=True)  16.3 us
    dot_general x12, matrix products, to_field(): jnp.einsum('nxc,cy->nxy', half_im, sin_tab, precision=precise)  14.4 us
    psum x1, blocking collectives, on_device(): summed = lax.psum(partial_grad, ('corner', 'kern'))  12.2 us
    dot_general x12, matrix products, to_field(): jnp.einsum('nxc,cy->nxy', half_re, sin_tab, precision=precise)  9.21 us
    dot_general x12, matrix products, to_field(): jnp.einsum('nxc,cy->nxy', half_re, cos_tab, precision=precise)  9.12 us
    dot_general x12, matrix products, to_field(): jnp.einsum('nxc,cy->nxy', half_im, cos_tab, precision=precise)  9.12 us
    dynamic_slice x30, local copies, waits for them, and re-layouts, on_device(): lax.scan(forward, jnp.zeros((local_tiles, P_SIZE, P_SIZE), jnp.float32),...  7.97 us
  transfers between devices with their start and end apart: 5, of which 3 were waited for; matrix products, arithmetic and copies ran while one was open for 8% of the time, Pallas kernels for 0%

profile of v1, /device:TPU:0, one launch (start us, length us, event | category | flops | bytes accessed | tf_op | source)
XLA Modules:
  0.0 203.3 jit_solution(12753898354974016477)
XLA Ops:
  7.2 3.1 %collective-permute-start = (bf16[1,256,256]{2,1,0:T(8,128)(2,1)}, bf16[1,256,256]{2,1,0:T(8,128)(2,1)S(1)}, u32[]{:S(2)}, u32[]{:S(2)}) collective-permute-start(bf16[1,256,256]{2,1,0:T(8,128)(2,1)} %param.13), channel_id=1, source_target_pairs={{0,4},{4,8},{8,12},{12,0},{1,5},{5,9},{9,13},{13,1},{2,6},{6,10},{... | collective-permute-start | bytes 393224 | tf_op jit(solution)/shard_map/ppermute | solution.py:113
  10.3 2.1 %collective-permute-start.1 = (bf16[1,256,256]{2,1,0:T(8,128)(2,1)}, bf16[1,256,256]{2,1,0:T(8,128)(2,1)S(1)}, u32[]{:S(2)}, u32[]{:S(2)}) collective-permute-start(bf16[1,256,256]{2,1,0:T(8,128)(2,1)} %param.13), channel_id=1, source_target_pairs={{0,12},{4,0},{8,4},{12,8},{1,13},{5,1},{9,5},{13,9},{2,14},{6,2},{... | collective-permute-start | bytes 393224 | tf_op jit(solution)/shard_map/ppermute | solution.py:116
  12.4 1.3 convolution_bitcast_fusion.3
  15.5 1.4 collective-permute-done
  17.4 3.4 %dynamic_update_slice.12 = bf16[4,256,256]{2,0,1:T(4,128)(2,1)S(1)} dynamic-update-slice(bf16[4,256,256]{2,0,1:T(4,128)(2,1)S(1)} %broadcast_in_dim.8, bf16[1,256,256]{2,0,1:T(2,128)(2,1)S(1)} %copy.30, s32[]{:T(128)S(6)} %select_n.140, s32[]{:T(128)} %constant.87.clone.1, s32[]{:T(128)} %constant.87.clone.1) | dynamic-update-slice | bytes 262148 | tf_op jit(solution)/shard_map/dynamic_update_slice | solution.py:108
  21.1 3.4 %dynamic_update_slice.13 = bf16[4,256,256]{2,0,1:T(4,128)(2,1)S(1)} dynamic-update-slice(bf16[4,256,256]{2,0,1:T(4,128)(2,1)S(1)} %dynamic_update_slice.12, bf16[1,256,256]{2,0,1:T(2,128)(2,1)S(1)} %copy.31, s32[]{:T(128)S(6)} %select_n.142, s32[]{:T(128)} %constant.87.clone.1, s32[]{:T(128)} %constant.87.clone.1) | dynamic-update-slice | bytes 262148 | tf_op jit(solution)/shard_map/dynamic_update_slice | solution.py:114
  24.7 3.4 %dynamic_update_slice.14 = bf16[4,256,256]{2,0,1:T(4,128)(2,1)S(1)} dynamic-update-slice(bf16[4,256,256]{2,0,1:T(4,128)(2,1)S(1)} %dynamic_update_slice.13, bf16[1,256,256]{2,0,1:T(2,128)(2,1)S(1)} %copy.32, s32[]{:T(128)S(6)} %select_n.144, s32[]{:T(128)} %constant.87.clone.1, s32[]{:T(128)} %constant.87.clone.1) | dynamic-update-slice | bytes 262148 | tf_op jit(solution)/shard_map/dynamic_update_slice | solution.py:119
  28.3 3.4 %dynamic_update_slice.15 = bf16[4,256,256]{2,0,1:T(4,128)(2,1)S(1)} dynamic-update-slice(bf16[4,256,256]{2,0,1:T(4,128)(2,1)S(1)} %dynamic_update_slice.14, bf16[1,256,256]{2,0,1:T(2,128)(2,1)S(1)} %copy.33, s32[]{:T(128)S(6)} %select_n.146, s32[]{:T(128)} %constant.87.clone.1, s32[]{:T(128)} %constant.87.clone.1) | dynamic-update-slice | bytes 262148 | tf_op jit(solution)/shard_map/dynamic_update_slice | solution.py:114
  36.0 38.0 %while.30 = (s32[]{:T(128)}, f32[2,256,256]{2,1,0:T(8,128)S(1)}, f32[6]{0:T(128)S(1)}, f32[6,32,32]{2,1,0:T(8,128)S(1)}, f32[2,32,32]{1,2,0:T(8,128)S(1)}, /*ind...) while((s32[]{:T(128)}, f32[2,256,256]{2,1,0:T(8,128)S(1)}, ...), condition=%wide.region_1.2_spmd.clone.clone.clone.clone, body=%wide.region_0.1_spmd.clone.clone.clone.clone.sunk | while | flops 228810752 | bytes 4981891 | solution.py:148
  37.0 0.8 fusion.461
  38.5 0.8 fusion.464
  39.3 0.8 fusion.465
  40.7 1.6 fusion.466
  43.3 0.8 fusion.461
  44.9 0.8 fusion.464
  45.6 0.8 fusion.465
  47.0 1.6 fusion.466
  49.6 0.8 fusion.461
  51.2 0.8 fusion.464
  52.0 0.8 fusion.465
  53.3 1.6 fusion.466
  56.0 0.8 fusion.461
  57.5 0.8 fusion.464
  58.3 0.8 fusion.465
  59.7 1.6 fusion.466
  62.3 0.8 fusion.461
  63.9 0.8 fusion.464
  64.6 0.8 fusion.465
  66.0 1.6 fusion.466
  68.6 0.8 fusion.461
  70.2 0.8 fusion.464
  71.0 0.8 fusion.465
  72.3 1.6 fusion.466
  74.0 0.8 copy-done.1
  75.7 19.7 %all-reduce.2.cloned.1.call-done = f32[2,256,256]{2,1,0:T(8,128)} async-done(((f32[2,256,256]{2,1,0:T(8,128)}), f32[2,256,256]{2,1,0:T(8,128)}) %all-reduce.2.cloned.1.call-update) | async-done | bytes 524304 | tf_op jit(solution)/shard_map/psum | solution.py:151
  95.4 1.3 multiply_multiply_fusion
  96.7 61.6 %while.31 = (s32[]{:T(128)}, f32[2,32,32]{2,1,0:T(8,128)S(1)}, f32[2,32,32]{2,1,0:T(8,128)S(1)}, f32[6]{0:T(128)S(1)}, f32[2,256,256]{2,1,0:T(8,128)S(1)}, /*ind...) while((s32[]{:T(128)}, f32[2,32,32]{2,1,0:T(8,128)S(1)}, ...), condition=%wide.region_4.5_spmd.clone.clone.clone.clone, body=%wide.region_3.4_spmd.clone.clone.clone.clone.sunk | while | flops 456050688 | bytes 7833771 | solution.py:164
  97.7 0.8 fusion.501
  100.5 0.8 fusion.502
  101.9 0.8 fusion.496
  102.6 0.8 fusion.499
  107.9 0.8 fusion.501
  110.8 0.8 fusion.502
  112.2 0.8 fusion.496
  112.9 0.8 fusion.499
  121.0 0.8 fusion.502
  122.4 0.8 fusion.496
  123.2 0.8 fusion.499
  131.3 0.8 fusion.502
  132.7 0.8 fusion.496
  133.5 0.8 fusion.499
  138.8 0.8 fusion.501
  141.6 0.8 fusion.502
  143.0 0.8 fusion.496
  143.7 0.8 fusion.499
  151.8 0.8 fusion.502
  153.2 0.8 fusion.496
  154.0 0.8 fusion.499
  158.3 12.2 %psum.15 = f32[2,2,32,32]{3,2,0,1:T(8,128)S(1)} all-reduce(f32[2,2,32,32]{3,2,0,1:T(8,128)S(1)} %pad_maximum_fusion.1), channel_id=1, replica_groups=mesh['region'=2,'tile'=4,'corner'=2,'kern'=2] {'corner','kern'}, use_global_device_ids=true, to_apply=%region_5.6 | all-reduce | flops 4096 | bytes 32768 | tf_op jit(solution)/shard_map/psum | solution.py:166
  173.8 0.8 fusion.217
  174.6 1.6 convolution_add_fusion.6
  176.1 16.3 %reduce-scatter.2.cloned.1.call-done = f32[1,2,32,32]{3,2,1,0:T(8,128)} async-done(((f32[4,2,32,32]{3,2,1,0:T(8,128)}), f32[1,2,32,32]{3,2,1,0:T(8,128)}) %reduce-scatter.2.cloned.1.call-update) | async-done | bytes 8208 | tf_op jit(solution)/shard_map/reduce_scatter | solution.py:179
  192.4 1.1 fusion.248
  195.2 1.3 fusion.189
  (213 shorter events, 66.9 us)
Async XLA Ops:
  7.2 7.4 %copy-start = (f32[1,12,2,32,32]{4,3,2,1,0:T(8,128)S(1)}, f32[1,12,2,32,32]{4,3,2,1,0:T(8,128)}, u32[]{:S(2)}) copy-start(f32[1,12,2,32,32]{4,3,2,1,0:T(8,128)} %param.17) | copy-start | bytes 294916
  7.2 6.6 %copy-start.2 = (bf16[2,256,256]{2,1,0:T(8,128)(2,1)S(1)}, bf16[2,256,256]{2,1,0:T(8,128)(2,1)}, u32[]{:S(2)}) copy-start(bf16[2,256,256]{2,1,0:T(8,128)(2,1)} %param.12) | copy-start | bytes 786436
  7.2 88.2 %all-reduce.2.cloned.1.call-start = ((), (), s32[]{:S(2)}) async-start(), calls=%async_computation.1 | async-start | bytes 1048576 | tf_op jit(solution)/shard_map/psum | solution.py:151
  7.2 9.6 %collective-permute-start = (bf16[1,256,256]{2,1,0:T(8,128)(2,1)}, bf16[1,256,256]{2,1,0:T(8,128)(2,1)S(1)}, u32[]{:S(2)}, u32[]{:S(2)}) collective-permute-start(bf16[1,256,256]{2,1,0:T(8,128)(2,1)} %param.13), channel_id=1, source_target_pairs={{0,4},{4,8},{8,12},{12,0},{1,5},{5,9},{9,13},{13,1},{2,6},{6,10},{... | collective-permute-start | bytes 393224 | tf_op jit(solution)/shard_map/ppermute | solution.py:113
  10.3 14.1 %collective-permute-start.1 = (bf16[1,256,256]{2,1,0:T(8,128)(2,1)}, bf16[1,256,256]{2,1,0:T(8,128)(2,1)S(1)}, u32[]{:S(2)}, u32[]{:S(2)}) collective-permute-start(bf16[1,256,256]{2,1,0:T(8,128)(2,1)} %param.13), channel_id=1, source_target_pairs={{0,12},{4,0},{8,4},{12,8},{1,13},{5,1},{9,5},{13,9},{2,14},{6,2},{... | collective-permute-start | bytes 393224 | tf_op jit(solution)/shard_map/ppermute | solution.py:116
  14.6 0.7 copy-start.6
  14.6 2.4 %copy-start.4 = (bf16[1,256,256]{2,1,0:T(8,128)(2,1)S(1)}, bf16[1,256,256]{2,1,0:T(8,128)(2,1)}, u32[]{:S(2)}) copy-start(bf16[1,256,256]{2,1,0:T(8,128)(2,1)} %param.13) | copy-start | bytes 393220
  16.9 11.2 %collective-permute-start.2 = (bf16[1,256,256]{2,1,0:T(8,128)(2,1)S(1)}, bf16[1,256,256]{2,1,0:T(8,128)(2,1)S(1)}, u32[]{:S(2)}, u32[]{:S(2)}) collective-permute-start(bf16[1,256,256]{2,1,0:T(8,128)(2,1)S(1)} %collective-permute-done), channel_id=1, source_target_pairs={{0,4},{4,8},{8,12},{12,0},{1,5},{5,9},{9,13},{13,1},{2,6},{6,10},{... | collective-permute-start | bytes 393224 | tf_op jit(solution)/shard_map/ppermute | solution.py:113
  17.4 3.4 %copy-start.8 = (f32[1,12]{1,0:T(1,128)S(1)}, f32[1,12]{1,0:T(1,128)}, u32[]{:S(2)}) copy-start(f32[1,12]{1,0:T(1,128)} %param.18) | copy-start | bytes 148
  28.3 3.4 %copy-start.5 = (s32[2]{0:T(128)S(1)}, s32[2]{0:T(128)}, u32[]{:S(2)}) copy-start(s32[2]{0:T(128)} %param.15) | copy-start | bytes 28
  74.0 0.8 copy-start.1
  74.0 21.4 %copy-start.3 = (bf16[2,256,256]{2,1,0:T(8,128)(2,1)S(1)}, bf16[2,256,256]{2,1,0:T(8,128)(2,1)}, u32[]{:S(2)}) copy-start(bf16[2,256,256]{2,1,0:T(8,128)(2,1)} %param.14) | copy-start | bytes 786436
  74.8 117.6 %reduce-scatter.2.cloned.1.call-start = ((), (), s32[]{:S(2)}) async-start(), calls=%async_computation.2 | async-start | bytes 163840 | tf_op jit(solution)/shard_map/reduce_scatter | solution.py:179
  192.4 1.2 copy-start.7
Sparse Core Ops, SparseCore 0:
  74.9 20.4 all-reduce.1
  173.1 19.2 reduce-scatter.1
